TPU v7x, 128 devices: a whole 4x4x4 slice. The times are simulated.
128 devices in a mesh: req: 32 (over x, y, core), tp: 4 (over z).
Axes of the slice: x: 4, y: 4, z: 4, core: 2. Of those that a mesh axis runs over, the one named last changes fastest.
Arguments:
- stream: bfloat16 [64, 64, 3584], P('req'), may hold values from -40 to 40
- queries: bfloat16 [64, 64, 3584], P('req', None, 'tp'), may hold values from -4 to 4
- key_new: bfloat16 [64, 64, 3584], P('req', None, 'tp'), may hold values from -18 to 18
- value_new: bfloat16 [64, 64, 3584], P('req', None, 'tp'), may hold values from -6 to 6
- cache_key: bfloat16 [64, 1024, 3584], P('req', None, 'tp'), may hold values from -5 to 5
- cache_value: bfloat16 [64, 1024, 3584], P('req', None, 'tp'), may hold values from -6 to 6
- cache_length: int32 [64], P('req'), may hold values from 64 to 1024, as said below
- parents: int32 [64, 64], P('req'), may hold values from -1 to 62, as said below
- accept: int32 [64, 8, 64], P('req'), may hold values from 0 to 1, as said below
- out_weight: bfloat16 [3584, 3584], P('tp'), may hold values from -0.75 to 0.75
- norm_gain: float32 [3584], replicated, may hold values from 0.1 to 1.9
- head_weight: bfloat16 [32000, 3584], P('req'), may hold values from -1 to 1
- candidate: int32 [64, 64], replicated, may hold values from 0 to 31999
- dealing: int32 [64], replicated, may hold values from 0 to 63, each once
Outputs:
- target_logprob: float32 [64, 64], P('req')
- accepted_state: bfloat16 [64, 8, 3584], P('req', None, 'tp')
Inputs may be any that keep to these rules, and one draw needn't show every extreme that they name: `cache_length`: every cache holds at least 64 live positions; in every draw some slot's cache is full. `parents`: node 0 is the root with parent -1; node t > 0 lies at depth (t - 1) // 9 + 1 and its parent lies one depth above it. `accept`: row a of a slot's matrix is one-hot on the node at depth a of the accepted path, which runs from the root down the slot's tree to some node; rows past the path's end are zero; in every draw some path ends at the deepest level.
All inputs are finite; a program needn't handle non-finite values.
Results may differ from a plain program's by a relative error of at most 0.012.
Values may be sent and summed in bfloat16 or wider, within the bound.
No kernel may reach another device: no remote copies, remote signals or barrier semaphores. Data moves between devices by JAX's collectives and lax.ppermute only.
A program may use at most 192 MiB of HBM per device.

v0:
```python
import jax
import jax.numpy as jnp
from jax import lax
from jax.sharding import PartitionSpec as P

HD = 224
ACC = 8
EPS = 1e-05
HIGH = lax.Precision.HIGHEST
block_limit = 512


def combined_all(value, axis, join):
    pieces = jax.tree.map(lambda part: lax.all_gather(part, axis), value)
    head = jax.tree.map(lambda part: part[0], pieces)
    tail = jax.tree.map(lambda part: part[1:], pieces)
    subtotal, _ = lax.scan(lambda subtotal, share: (join(subtotal, share), None), head, tail)
    return subtotal


def ancestry(parents):
    node_count = parents.shape[-1]
    node_ids = jnp.arange(node_count, dtype=jnp.int32)
    stride_map = (parents[..., :, None] == node_ids).astype(jnp.float32)
    reached = jnp.broadcast_to(jnp.eye(node_count, dtype=jnp.float32), stride_map.shape) > 0.5
    for doubling in range((ACC - 1).bit_length()):
        further = lax.optimization_barrier(
            jnp.einsum("rtk,rku->rtu", reached.astype(jnp.float32), stride_map, precision=HIGH)
        )
        reached = jnp.logical_or(reached, further > 0.5)
        stride_map = jnp.einsum("rtk,rku->rtu", stride_map, stride_map, precision=HIGH)
    return reached


def combine_stats(earlier, later):
    joint_max = jnp.maximum(earlier[0], later[0])
    joint_sum = earlier[1] * jnp.exp(earlier[0] - joint_max) + later[1] * jnp.exp(
        later[0] - joint_max
    )
    return (joint_max, joint_sum, earlier[2] + later[2])


def vocab_stats(logits, vocab_ids, wanted, along):
    row_max = jnp.max(logits, axis=along)
    row_sum = jnp.sum(jnp.exp(logits - jnp.expand_dims(row_max, along)), axis=along)
    matches = jnp.expand_dims(vocab_ids, 1 - along) == jnp.expand_dims(wanted, along)
    picked = jnp.sum(jnp.where(matches, logits, 0.0), axis=along)
    return (row_max, row_sum, picked)


def local(
    stream,
    queries,
    key_new,
    value_new,
    cache_key,
    cache_value,
    cache_length,
    parents,
    accept,
    out_weight,
    norm_gain,
    head_weight,
    candidate,
    dealing,
):
    slots, tree_size, qwidth = queries.shape
    model_width = stream.shape[2]
    heads_loc = qwidth // HD
    n_tp = lax.axis_size("tp")
    n_req = lax.axis_size("req")
    tp_id = lax.axis_index("tp")
    req_id = lax.axis_index("req")
    score_scale = HD ** (-0.5)
    query_rows = queries.reshape(slots, tree_size, heads_loc, HD)
    tree_keys = key_new.reshape(slots, tree_size, heads_loc, HD)
    tree_values = value_new.reshape(slots, tree_size, heads_loc, HD)
    visible = ancestry(parents)
    tree_scores = (
        jnp.einsum("rthd,rkhd->rhtk", query_rows, tree_keys, preferred_element_type=jnp.float32)
        * score_scale
    )
    tree_scores = jnp.where(visible[:, None], tree_scores, -jnp.inf)
    running_max = jnp.max(tree_scores, axis=3)
    weights = jnp.exp(tree_scores - running_max[..., None])
    running_sum = jnp.sum(weights, axis=3)
    running_out = jnp.einsum(
        "rhtk,rkhd->rhtd",
        weights.astype(jnp.bfloat16),
        tree_values,
        preferred_element_type=jnp.float32,
    )
    cache_cap = cache_key.shape[1]
    block_rows = min(block_limit, cache_cap)
    block_count = (jnp.max(cache_length) + block_rows - 1) // block_rows

    def visit_block(block_index, folded):
        old_max, old_sum, old_out = folded
        offset = block_index * block_rows
        past_keys = lax.dynamic_slice_in_dim(cache_key, offset, block_rows, 1).reshape(
            slots, block_rows, heads_loc, HD
        )
        past_values = lax.dynamic_slice_in_dim(cache_value, offset, block_rows, 1).reshape(
            slots, block_rows, heads_loc, HD
        )
        scores = (
            jnp.einsum("rthd,rkhd->rhtk", query_rows, past_keys, preferred_element_type=jnp.float32)
            * score_scale
        )
        live_mask = (offset + jnp.arange(block_rows, dtype=jnp.int32))[None, :] < cache_length[
            :, None
        ]
        scores = jnp.where(live_mask[:, None, None, :], scores, -jnp.inf)
        new_max = jnp.maximum(old_max, jnp.max(scores, axis=3))
        shrink = jnp.exp(old_max - new_max)
        block_weights = jnp.exp(scores - new_max[..., None])
        new_sum = old_sum * shrink + jnp.sum(block_weights, axis=3)
        contribution = lax.optimization_barrier(
            jnp.einsum(
                "rhtk,rkhd->rhtd",
                block_weights.astype(jnp.bfloat16),
                past_values,
                preferred_element_type=jnp.float32,
            )
        )
        new_out = old_out * shrink[..., None] + contribution
        return (new_max, new_sum, new_out)

    running_max, running_sum, running_out = lax.fori_loop(
        0, block_count, visit_block, (running_max, running_sum, running_out)
    )
    attention = (running_out / running_sum[..., None]).astype(jnp.bfloat16)
    attention_rows = attention.transpose(0, 2, 1, 3).reshape(slots * tree_size, qwidth)
    flat_stream = stream.reshape(slots * tree_size, model_width)
    rows_all = slots * tree_size
    quarter = rows_all // n_tp
    dslice = model_width // n_tp
    partial_out = jnp.dot(attention_rows, out_weight, preferred_element_type=jnp.float32)
    summed = lax.psum_scatter(
        partial_out.astype(jnp.bfloat16), "tp", scatter_dimension=1, tiled=True
    ).astype(jnp.float32)
    own_stream = lax.dynamic_slice_in_dim(flat_stream, tp_id * dslice, dslice, 1)
    post_rows = (own_stream.astype(jnp.float32) + summed).astype(jnp.bfloat16)
    post_float = post_rows.astype(jnp.float32)
    square = jnp.sum(post_float * post_float, axis=1)
    energy = lax.psum(square, "tp")
    inverse = lax.rsqrt(energy / model_width + EPS)
    part_gain = lax.dynamic_slice_in_dim(norm_gain, tp_id * dslice, dslice, 0)
    normed_slice = (post_float * inverse[:, None] * part_gain[None, :]).astype(jnp.bfloat16)
    compact = jnp.einsum(
        "sat,std->sad",
        accept.astype(jnp.bfloat16),
        post_rows.reshape(slots, tree_size, dslice),
        preferred_element_type=jnp.float32,
    ).astype(jnp.bfloat16)
    normed = lax.all_to_all(normed_slice, "tp", split_axis=0, concat_axis=1, tiled=True)
    vocab_loc = head_weight.shape[0]
    wanted_rows = lax.dynamic_slice_in_dim(
        candidate.reshape(n_req, rows_all), tp_id * quarter, quarter, 1
    ).reshape(-1)
    vocab_ids = req_id * vocab_loc + jnp.arange(vocab_loc, dtype=jnp.int32)
    logits = lax.dot_general(
        lax.all_gather(normed, "req", axis=0, tiled=True),
        head_weight,
        (((1,), (1,)), ((), ())),
        preferred_element_type=jnp.float32,
    )
    found_stats = vocab_stats(logits, vocab_ids, wanted_rows, 1)
    local_stats = tuple((after_part for after_part in found_stats))
    merged = combined_all((local_stats[0], local_stats[1], local_stats[2]), "req", combine_stats)
    all_stats = (
        lax.all_gather(merged[0], "tp", axis=0, tiled=True),
        lax.all_gather(merged[1], "tp", axis=0, tiled=True),
        lax.all_gather(merged[2], "tp", axis=0, tiled=True),
    )
    row_max, row_sum, picked = tuple(
        (
            member.reshape(n_tp, n_req, quarter).transpose(1, 0, 2).reshape(-1)
            for member in all_stats
        )
    )
    logprob = (picked - row_max - jnp.log(row_sum)).reshape(-1, tree_size)
    own_requests = req_id * slots + jnp.arange(slots, dtype=jnp.int32)
    selector = dealing[None, :] == own_requests[:, None]
    target_logprob = jnp.dot(selector.astype(jnp.float32), logprob, precision=HIGH)
    home_states = lax.all_gather(compact, "req", axis=0, tiled=True)
    accepted_state = jnp.einsum(
        "ks,sad->kad",
        selector.astype(jnp.bfloat16),
        home_states,
        preferred_element_type=jnp.float32,
    ).astype(jnp.bfloat16)
    return (target_logprob, accepted_state)


def solution(mesh):
    placed = (
        P("req", None, None),
        P("req", None, "tp"),
        P("req", None, "tp"),
        P("req", None, "tp"),
        P("req", None, "tp"),
        P("req", None, "tp"),
        P("req"),
        P("req", None),
        P("req", None, None),
        P("tp", None),
        P(),
        P("req", None),
        P(),
        P(),
    )
    return jax.shard_map(
        local,
        mesh=mesh,
        in_specs=placed,
        out_specs=(P("req", None), P("req", None, "tp")),
        check_vma=False,
    )
```

profile of v0, /device:TPU:0, one launch (start us, length us, event | category | flops | bytes accessed | tf_op | source)
XLA Modules:
  0.0 275.6 jit_solution(6451548967636028759)
XLA Ops:
  7.2 0.0 reduce-scatter.4.cloned.1.call-start
  7.2 1.4 reduce_max.37
  9.3 1.0 fusion.21
  10.3 0.2 fusion.38
  10.5 0.9 fusion.22
  11.4 0.2 fusion.37
  11.6 0.2 fusion.39
  11.8 0.1 copy.47
  11.9 1.2 reshape.97
  13.1 0.7 copy.48
  13.9 1.2 reshape.98
  15.1 1.2 reshape.99
  16.3 0.2 fusion.35
  16.5 0.1 fusion.18
  16.6 0.3 fusion.13
  16.9 12.5 %while.28 = (s32[]{:T(128)}, f32[2,4,64]{2,1,0:T(4,128)S(1)}, f32[2,4,64]{2,1,0:T(4,128)S(1)}, f32[2,4,64,224]{3,2,1,0:T(8,128)S(1)}, s32[]{:T(128)}, /*index=5*...) while((s32[]{:T(128)}, f32[2,4,64]{2,1,0:T(4,128)S(1)}, ...), condition=%wide.region_6.7_spmd, body=%wide.region_3.6_spmd.sunk | while | flops 236947968 | bytes 23599292 | solution.py:129
  16.9 0.1 broadcast_compare_fusion.2
  17.0 4.1 %constant_dynamic-slice_fusion.9 = (bf16[2,512,896]{2,1,0:T(8,128)(2,1)}, bf16[2,512,896]{2,1,0:T(8,128)(2,1)}) fusion(bf16[2,1024,896]{2,1,0:T(8,128)(2,1)} %get-tuple-element.346, s32[]{:T(128)S(6)} %select_n.42, bf16[2,1024,896]{2,1,0:T(8,128)(2,1)} %get-tuple-element.344), kind=kLoop, calls=%fused_computation.13.clone.1 | loop fusion | bytes 7340036 | tf_op jit(solution)/shard_map/while/body/dynamic_slice | solution.py:103
  21.1 2.7 copy.80
  23.9 1.5 fusion.66
  25.4 0.3 fusion.67
  25.8 2.8 copy.81
  28.5 0.7 fusion.68
  29.2 0.2 multiply_add_fusion.7
  29.4 0.1 fusion.16
  29.6 0.2 copy.55
  29.8 0.2 reshape.100
  30.0 4.0 %convolution_convert_fusion = bf16[128,3584]{1,0:T(8,128)(2,1)S(1)} fusion(bf16[128,896]{1,0:T(8,128)(2,1)S(1)} %reshape.100, bf16[896,3584]{1,0:T(8,128)(2,1)} %param.27), kind=kOutput, calls=%fused_computation.19 | convolution fusion | flops 822542336 | bytes 7569408 | tf_op jit(solution)/shard_map/dot_general | solution.py:138
  34.0 0.0 copy-start
  34.0 0.0 copy-start.2
  34.0 0.0 copy-start.3
  34.0 1.3 copy.61
  35.3 0.0 reduce-scatter.4.cloned.1.call-update
  35.3 0.0 all-gather.5.cloned.1.call-start
  35.4 0.8 dynamic_slice.26
  36.1 37.4 %reduce-scatter.4.cloned.1.call-done = bf16[896,128]{1,0:T(8,128)(2,1)} async-done(((bf16[3584,128]{1,0:T(8,128)(2,1)}), bf16[896,128]{1,0:T(8,128)(2,1)}) %reduce-scatter.4.cloned.1.call-update) | async-done | bytes 229392
  73.5 1.1 copy.62
  74.6 1.1 fusion.10
  75.7 8.0 %psum.7 = f32[128]{0:T(128)S(1)} all-reduce(f32[128]{0:T(128)S(1)} %get-tuple-element.177), channel_id=1, replica_groups=mesh['req'=32,'tp'=4] {'tp'}, use_global_device_ids=true, to_apply=%region_9.10 | all-reduce | flops 128 | bytes 1024 | tf_op jit(solution)/shard_map/psum | solution.py:146
  83.7 0.1 fusion.12
  83.9 9.3 %all_to_all.19 = bf16[4,32,896]{2,1,0:T(8,128)(2,1)S(1)} all-to-all(bf16[4,32,896]{2,1,0:T(8,128)(2,1)S(1)} %bitcast.79), channel_id=1, replica_groups=mesh['req'=32,'tp'=4] {'tp'}, dimensions={0} | all-to-all | bytes 458752 | tf_op jit(solution)/shard_map/all_to_all | solution.py:156
  93.2 0.7 copy.65
  93.9 0.0 all-gather.5.cloned.1.call-update
  93.9 0.1 reshape.101
  94.0 0.1 constant_dynamic-slice_fusion.5
  94.1 0.1 eq.54
  94.2 0.1 fusion.8
  94.3 25.4 %all_gather.43 = bf16[64,8,896]{2,1,0:T(8,128)(2,1)S(1)} all-gather(bf16[2,8,896]{2,1,0:T(8,128)(2,1)S(1)} %fusion.8), channel_id=1, replica_groups=mesh['req'=32,'tp'=4] {'req'}, dimensions={0}, use_global_device_ids=true | all-gather | bytes 946176 | tf_op jit(solution)/shard_map/all_gather | solution.py:186
  119.7 0.3 convolution_convert_fusion.1
  120.0 0.6 copy.59
  120.7 23.6 %all-gather.5.cloned.1.call-done = bf16[1024,3584]{1,0:T(8,128)(2,1)} async-done(((bf16[32,3584]{1,0:T(8,128)(2,1)}), bf16[1024,3584]{1,0:T(8,128)(2,1)}) %all-gather.5.cloned.1.call-update) | async-done | bytes 7340048 | tf_op jit(solution)/shard_map/all_gather | solution.py:163
  144.2 12.1 %fusion.36 = (f32[1024]{0:T(1024)S(1)}, f32[1024,1000]{0,1:T(8,128)S(1)}) fusion(bf16[1024,3584]{1,0:T(8,128)(2,1)} %all-gather.5.cloned.1.call-done, bf16[1000,3584]{1,0:T(8,128)(2,1)} %param.29), kind=kOutput, calls=%fused_computation.70 | convolution fusion | flops 7341054976 | bytes 18608128 | tf_op jit(solution)/shard_map/dot_general | solution.py:162
  156.3 1.4 select_reduce_fusion
  157.7 24.1 %all-gather.2 = f32[32768]{0:T(1024)S(1)} all-gather(f32[1024]{0:T(1024)S(1)} %get-tuple-element.139), channel_id=4, replica_groups=mesh['req'=32,'tp'=4] {'req'}, dimensions={0}, use_global_device_ids=true | all-gather | bytes 135168 | tf_op jit(solution)/shard_map/all_gather | solution.py:14
  181.8 22.7 %all-gather = f32[32768]{0:T(1024)S(1)} all-gather(f32[1024]{0:T(1024)S(1)} %get-tuple-element.187), channel_id=2, replica_groups=mesh['req'=32,'tp'=4] {'req'}, dimensions={0}, use_global_device_ids=true | all-gather | bytes 135168 | tf_op jit(solution)/shard_map/all_gather | solution.py:14
  204.5 23.8 %all-gather.1 = f32[32768]{0:T(1024)S(1)} all-gather(f32[1024]{0:T(1024)S(1)} %get-tuple-element.140), channel_id=3, replica_groups=mesh['req'=32,'tp'=4] {'req'}, dimensions={0}, use_global_device_ids=true | all-gather | bytes 135168 | tf_op jit(solution)/shard_map/all_gather | solution.py:14
  228.4 2.8 %while.29 = (s32[]{:T(128)}, f32[1024]{0:T(1024)S(1)}, f32[1024]{0:T(1024)S(1)}, f32[1024]{0:T(1024)S(1)}, f32[31,1024]{1,0:T(8,128)S(1)}, /*index=5*/f32[31,1024]{1,0:T(8,128)S(1)}, f32[31,1024]{1,0:T(8,128)S(1)}, s32[]{:T(128)}) while((s32[]{:T(128)}, f32[1024]{0:T(1024)S(1)}, f32[1024]{0:T(1024)S(1)}, f32[1024]{0:T(1024)S(1)}, ...), condition=%wide.region_14.15_spmd, body=%wide.region_13.14_spmd.sunk | while | flops 7170 | bytes 61541 | solution.py:17
  231.2 12.5 %all_gather.40 = f32[4096]{0:T(1024)S(1)} all-gather(f32[1024]{0:T(1024)S(1)} %get-tuple-element.92), channel_id=1, replica_groups=mesh['req'=32,'tp'=4] {'tp'}, dimensions={0}, use_global_device_ids=true | all-gather | bytes 20480 | tf_op jit(solution)/shard_map/all_gather | solution.py:174
  243.7 12.0 %all_gather.41 = f32[4096]{0:T(1024)S(1)} all-gather(f32[1024]{0:T(1024)S(1)} %get-tuple-element.93), channel_id=1, replica_groups=mesh['req'=32,'tp'=4] {'tp'}, dimensions={0}, use_global_device_ids=true | all-gather | bytes 20480 | tf_op jit(solution)/shard_map/all_gather | solution.py:172
  255.7 12.0 %all_gather.42 = f32[4096]{0:T(1024)S(1)} all-gather(f32[1024]{0:T(1024)S(1)} %get-tuple-element.94), channel_id=1, replica_groups=mesh['req'=32,'tp'=4] {'tp'}, dimensions={0}, use_global_device_ids=true | all-gather | bytes 20480 | tf_op jit(solution)/shard_map/all_gather | solution.py:173
  267.8 0.1 sub.68
  267.8 0.1 copy.57
  267.9 0.1 sub.70
  268.0 0.8 fusion.27
  (149 shorter events, 1.7 us)
Async XLA Ops:
  7.2 9.7 %copy-start.1 = (s32[2]{0:T(128)S(1)}, s32[2]{0:T(128)}, u32[]{:S(2)}) copy-start(s32[2]{0:T(128)} %param.24) | copy-start | bytes 28
  7.2 66.4 %reduce-scatter.4.cloned.1.call-start = ((), (), s32[]{:S(2)}) async-start(), calls=%async_computation.3 | async-start | bytes 1146880
  34.0 60.0 %copy-start = (s32[64,64]{1,0:T(8,128)S(1)}, s32[64,64]{1,0:T(8,128)}, u32[]{:S(2)}) copy-start(s32[64,64]{1,0:T(8,128)} %param.30) | copy-start | bytes 49156
  34.0 60.2 %copy-start.2 = (s32[2,8,64]{2,1,0:T(8,128)S(1)}, s32[2,8,64]{2,1,0:T(8,128)}, u32[]{:S(2)}) copy-start(s32[2,8,64]{2,1,0:T(8,128)} %param.26) | copy-start | bytes 12292
  34.0 85.8 %copy-start.3 = (s32[64]{0:T(128)S(1)}, s32[64]{0:T(128)}, u32[]{:S(2)}) copy-start(s32[64]{0:T(128)} %param.31) | copy-start | bytes 772
  35.3 108.9 %all-gather.5.cloned.1.call-start = ((), (), s32[]{:S(2)}) async-start(), calls=%async_computation.2 | async-start | bytes 7569408 | tf_op jit(solution)/shard_map/all_gather | solution.py:163
Sparse Core Ops, SparseCore 0:
  35.4 38.0 reduce-scatter.3
  94.1 50.1 all-gather.4
where the time goes:
time: 276 us
  blocking collectives  150 us (54%)
  waiting for transfers between devices  61 us (22%)
  matrix products  22.3 us (8%)
  local copies, waits for them, and re-layouts  20.5 us (7%)
  between operations  15 us (5%)
  other arithmetic  5.41 us (2%)
    all_gather x3, blocking collectives, combined_all(): pieces = jax.tree.map(lambda part: lax.all_gather(part, axis), value)  70.6 us
    unnamed x3, waiting for transfers between devices  37.4 us
    all_gather x1, blocking collectives, local(): home_states = lax.all_gather(compact, 'req', axis=0, tiled=True)  25.4 us
    all_gather x1, waiting for transfers between devices, local(): lax.all_gather(normed, 'req', axis=0, tiled=True)  23.6 us
    all_gather x1, blocking collectives, local(): lax.all_gather(merged[2], 'tp', axis=0, tiled=True)  12.5 us
    dot_general x1, matrix products, local(): lax.dot_general(lax.all_gather(normed, 'req', axis=0, tiled=True), head_w...  12.1 us
    all_gather x1, blocking collectives, local(): lax.all_gather(merged[0], 'tp', axis=0, tiled=True)  12 us
    all_gather x1, blocking collectives, local(): lax.all_gather(merged[1], 'tp', axis=0, tiled=True)  12 us
  transfers between devices with their start and end apart: 2, of which 2 were waited for; matrix products, arithmetic and copies ran while one was open for 1% of the time, Pallas kernels for 0%

commit v1 on v0

--- a/solution.py
+++ b/solution.py
@@ -1,3 +1,4 @@
+import functools
 import jax
 import jax.numpy as jnp
 from jax import lax
@@ -8,6 +9,33 @@
 EPS = 1e-05
 HIGH = lax.Precision.HIGHEST
 block_limit = 512
+
+
+def words_perform(work_x, axis_k):
+    piece_out = lax.axis_size("tp")
+    y1, answer, z_new = (piece_out, lax.axis_index("tp"), work_x.shape[axis_k])
+    shelf = tuple(((p, (p + 1) % y1) for p in range(y1)))
+    long_array = jnp.zeros(
+        (*work_x.shape[:axis_k], y1 * z_new, *work_x.shape[axis_k + 1 :]), work_x.dtype
+    )
+    long_array = lax.dynamic_update_slice_in_dim(long_array, work_x, answer * z_new, axis=axis_k)
+    fields = tuple(((p, (p - 1) % y1) for p in range(y1)))
+    state_now = y1 // 2
+    z = response = work_x
+    for s in range(1, state_now + 1):
+        z = lax.ppermute(z, "tp", shelf)
+        long_array = lax.dynamic_update_slice_in_dim(
+            long_array, z, (answer - s) % y1 * z_new, axis=axis_k
+        )
+        if s < y1 - state_now:
+            response = lax.ppermute(response, "tp", fields)
+            long_array = lax.dynamic_update_slice_in_dim(
+                long_array, response, (answer + s) % y1 * z_new, axis=axis_k
+            )
+    return long_array
+
+
+place_shelves_on = functools.partial(words_perform, axis_k=0)
 
 
 def combined_all(value, axis, join):
@@ -169,7 +197,7 @@
     local_stats = tuple((after_part for after_part in found_stats))
     merged = combined_all((local_stats[0], local_stats[1], local_stats[2]), "req", combine_stats)
     all_stats = (
-        lax.all_gather(merged[0], "tp", axis=0, tiled=True),
+        place_shelves_on(merged[0]),
         lax.all_gather(merged[1], "tp", axis=0, tiled=True),
         lax.all_gather(merged[2], "tp", axis=0, tiled=True),
     )

time: 276 us -> 269 us (0.975)
  blocking collectives: 150 us -> 137 us
  starting transfers between devices: 0.08 us -> 3.91 us
    all_gather x1 -> x0, blocking collectives: 12 us -> none  [local(): lax.all_gather(merged[0], 'tp', axis=0, tiled=True)]
    ppermute x0 -> x3, starting transfers between devices: none -> 3.83 us  [the longest x2 2.15 us: words_perform(): z = lax.ppermute(z, 'tp', shelf)]
  transfers between devices with their start and end apart: 2 -> 5, of which waited for: 2 -> 2; matrix products, arithmetic and copies ran while one was open for 1% -> 1% of each run, Pallas kernels for 0% -> 0%
where the time goes in v1:
time: 269 us; the launch traced here: 268 us
  blocking collectives  137 us (51%)
  waiting for transfers between devices  61 us (23%)
  matrix products  22.3 us (8%)
  local copies, waits for them, and re-layouts  21.4 us (8%)
  between operations  15.1 us (6%)
  other arithmetic  5.42 us (2%)
  starting transfers between devices  3.91 us (1%)
    all_gather x3, blocking collectives, combined_all(): pieces = jax.tree.map(lambda part: lax.all_gather(part, axis), value)  70.6 us
    unnamed x3, waiting for transfers between devices  37.4 us
    all_gather x1, blocking collectives, local(): home_states = lax.all_gather(compact, 'req', axis=0, tiled=True)  25.4 us
    all_gather x1, waiting for transfers between devices, local(): lax.all_gather(normed, 'req', axis=0, tiled=True)  23.5 us
    dot_general x1, matrix products, local(): lax.dot_general(lax.all_gather(normed, 'req', axis=0, tiled=True), head_w...  12.1 us
    all_gather x1, blocking collectives, local(): lax.all_gather(merged[2], 'tp', axis=0, tiled=True)  12 us
    all_gather x1, blocking collectives, local(): lax.all_gather(merged[1], 'tp', axis=0, tiled=True)  12 us
    all_to_all x1, blocking collectives, local(): lax.all_to_all(normed_slice, 'tp', split_axis=0, concat_axis=1, tiled=True)  9.35 us
  transfers between devices with their start and end apart: 5, of which 2 were waited for; matrix products, arithmetic and copies ran while one was open for 1% of the time, Pallas kernels for 0%

profile of v1, /device:TPU:0, one launch (start us, length us, event | category | flops | bytes accessed | tf_op | source)
XLA Modules:
  0.0 267.8 jit_solution(12670442148931357687)
XLA Ops:
  7.2 1.4 reduce_max.37
  9.3 1.0 fusion.21
  10.3 0.2 fusion.38
  10.5 0.9 fusion.22
  11.4 0.2 fusion.37
  11.6 0.2 fusion.39
  11.8 0.1 copy.47
  11.9 1.2 reshape.97
  13.1 0.7 copy.48
  13.9 1.2 reshape.98
  15.1 1.2 reshape.99
  16.3 0.2 fusion.35
  16.5 0.1 fusion.18
  16.6 0.3 fusion.13
  16.9 12.5 %while.28 = (s32[]{:T(128)}, f32[2,4,64]{2,1,0:T(4,128)S(1)}, f32[2,4,64]{2,1,0:T(4,128)S(1)}, f32[2,4,64,224]{3,2,1,0:T(8,128)S(1)}, s32[]{:T(128)}, /*index=5*...) while((s32[]{:T(128)}, f32[2,4,64]{2,1,0:T(4,128)S(1)}, ...), condition=%wide.region_6.7_spmd, body=%wide.region_3.6_spmd.sunk | while | flops 236947968 | bytes 23599292 | solution.py:157
  16.9 0.1 broadcast_compare_fusion.2
  17.0 4.1 %constant_dynamic-slice_fusion.9 = (bf16[2,512,896]{2,1,0:T(8,128)(2,1)}, bf16[2,512,896]{2,1,0:T(8,128)(2,1)}) fusion(bf16[2,1024,896]{2,1,0:T(8,128)(2,1)} %get-tuple-element.346, s32[]{:T(128)S(6)} %select_n.75, bf16[2,1024,896]{2,1,0:T(8,128)(2,1)} %get-tuple-element.344), kind=kLoop, calls=%fused_computation.13.clone.1 | loop fusion | bytes 7340036 | tf_op jit(solution)/shard_map/while/body/dynamic_slice | solution.py:131
  21.1 2.7 %copy.80 = bf16[2,512,896]{1,2,0:T(8,128)(2,1)S(1)} copy(bf16[2,512,896]{2,1,0:T(8,128)(2,1)} %get-tuple-element.295) | data formatting | bytes 3670016 | tf_op jit(solution)/shard_map/while/body/dynamic_slice | solution.py:128
  23.9 1.5 fusion.66
  25.4 0.3 fusion.67
  25.8 2.8 %copy.81 = bf16[2,512,896]{1,2,0:T(8,128)(2,1)S(1)} copy(bf16[2,512,896]{2,1,0:T(8,128)(2,1)} %get-tuple-element.300) | data formatting | bytes 3670016 | tf_op jit(solution)/shard_map/while/body/dynamic_slice | solution.py:131
  28.5 0.7 fusion.68
  29.2 0.2 multiply_add_fusion.7
  29.4 0.1 fusion.16
  29.6 0.2 copy.55
  29.8 0.2 reshape.100
  30.0 4.0 %convolution_convert_fusion = bf16[128,3584]{1,0:T(8,128)(2,1)S(1)} fusion(bf16[128,896]{1,0:T(8,128)(2,1)S(1)} %reshape.100, bf16[896,3584]{1,0:T(8,128)(2,1)} %param.27), kind=kOutput, calls=%fused_computation.19 | convolution fusion | flops 822542336 | bytes 7569408 | tf_op jit(solution)/shard_map/dot_general | solution.py:166
  34.0 1.3 copy.61
  35.3 0.0 all-gather.5.cloned.1.call-start
  35.4 0.8 dynamic_slice.26
  36.1 37.4 %reduce-scatter.4.cloned.1.call-done = bf16[896,128]{1,0:T(8,128)(2,1)} async-done(((bf16[3584,128]{1,0:T(8,128)(2,1)}), bf16[896,128]{1,0:T(8,128)(2,1)}) %reduce-scatter.4.cloned.1.call-update) | async-done | bytes 229392
  73.5 1.1 copy.62
  74.6 1.1 fusion.10
  75.7 8.0 %psum.7 = f32[128]{0:T(128)S(1)} all-reduce(f32[128]{0:T(128)S(1)} %get-tuple-element.177), channel_id=1, replica_groups=mesh['req'=32,'tp'=4] {'tp'}, use_global_device_ids=true, to_apply=%region_9.10 | all-reduce | flops 128 | bytes 1024 | tf_op jit(solution)/shard_map/psum | solution.py:174
  83.7 0.1 fusion.12
  83.9 9.3 %all_to_all.19 = bf16[4,32,896]{2,1,0:T(8,128)(2,1)S(1)} all-to-all(bf16[4,32,896]{2,1,0:T(8,128)(2,1)S(1)} %bitcast.79), channel_id=1, replica_groups=mesh['req'=32,'tp'=4] {'tp'}, dimensions={0} | all-to-all | bytes 458752 | tf_op jit(solution)/shard_map/all_to_all | solution.py:184
  93.2 0.7 copy.65
  94.0 0.1 reshape.101
  94.1 0.1 constant_dynamic-slice_fusion.5
  94.2 0.1 eq.58
  94.2 0.1 fusion.8
  94.4 25.4 %all_gather.39 = bf16[64,8,896]{2,1,0:T(8,128)(2,1)S(1)} all-gather(bf16[2,8,896]{2,1,0:T(8,128)(2,1)S(1)} %fusion.8), channel_id=1, replica_groups=mesh['req'=32,'tp'=4] {'req'}, dimensions={0}, use_global_device_ids=true | all-gather | bytes 946176 | tf_op jit(solution)/shard_map/all_gather | solution.py:214
  119.8 0.3 convolution_convert_fusion.1
  120.1 0.6 copy.59
  120.7 23.5 %all-gather.5.cloned.1.call-done = bf16[1024,3584]{1,0:T(8,128)(2,1)} async-done(((bf16[32,3584]{1,0:T(8,128)(2,1)}), bf16[1024,3584]{1,0:T(8,128)(2,1)}) %all-gather.5.cloned.1.call-update) | async-done | bytes 7340048 | tf_op jit(solution)/shard_map/all_gather | solution.py:191
  144.2 12.1 %fusion.36 = (f32[1024]{0:T(1024)S(1)}, f32[1024,1000]{0,1:T(8,128)S(1)}) fusion(bf16[1024,3584]{1,0:T(8,128)(2,1)} %all-gather.5.cloned.1.call-done, bf16[1000,3584]{1,0:T(8,128)(2,1)} %param.29), kind=kOutput, calls=%fused_computation.70 | convolution fusion | flops 7341054976 | bytes 18608128 | tf_op jit(solution)/shard_map/dot_general | solution.py:190
  156.3 1.4 select_reduce_fusion
  157.7 24.1 %all-gather.2 = f32[32768]{0:T(1024)S(1)} all-gather(f32[1024]{0:T(1024)S(1)} %get-tuple-element.139), channel_id=4, replica_groups=mesh['req'=32,'tp'=4] {'req'}, dimensions={0}, use_global_device_ids=true | all-gather | bytes 135168 | tf_op jit(solution)/shard_map/all_gather | solution.py:42
  181.8 22.7 %all-gather = f32[32768]{0:T(1024)S(1)} all-gather(f32[1024]{0:T(1024)S(1)} %get-tuple-element.187), channel_id=2, replica_groups=mesh['req'=32,'tp'=4] {'req'}, dimensions={0}, use_global_device_ids=true | all-gather | bytes 135168 | tf_op jit(solution)/shard_map/all_gather | solution.py:42
  204.5 23.8 %all-gather.1 = f32[32768]{0:T(1024)S(1)} all-gather(f32[1024]{0:T(1024)S(1)} %get-tuple-element.140), channel_id=3, replica_groups=mesh['req'=32,'tp'=4] {'req'}, dimensions={0}, use_global_device_ids=true | all-gather | bytes 135168 | tf_op jit(solution)/shard_map/all_gather | solution.py:42
  228.4 2.8 %while.29 = (s32[]{:T(128)}, f32[1024]{0:T(1024)S(1)}, f32[1024]{0:T(1024)S(1)}, f32[1024]{0:T(1024)S(1)}, f32[31,1024]{1,0:T(8,128)S(1)}, /*index=5*/f32[31,1024]{1,0:T(8,128)S(1)}, f32[31,1024]{1,0:T(8,128)S(1)}, s32[]{:T(128)}) while((s32[]{:T(128)}, f32[1024]{0:T(1024)S(1)}, f32[1024]{0:T(1024)S(1)}, f32[1024]{0:T(1024)S(1)}, ...), condition=%wide.region_14.15_spmd, body=%wide.region_13.14_spmd.sunk | while | flops 7170 | bytes 61541 | solution.py:45
  231.2 1.6 collective-permute-start
  232.9 1.7 collective-permute-start.1
  234.6 0.2 dynamic_update_slice.12
  234.7 12.0 %all_gather.37 = f32[4096]{0:T(1024)S(1)} all-gather(f32[1024]{0:T(1024)S(1)} %get-tuple-element.92), channel_id=1, replica_groups=mesh['req'=32,'tp'=4] {'tp'}, dimensions={0}, use_global_device_ids=true | all-gather | bytes 20480 | tf_op jit(solution)/shard_map/all_gather | solution.py:202
  246.7 0.5 collective-permute-start.2
  247.3 12.0 %all_gather.38 = f32[4096]{0:T(1024)S(1)} all-gather(f32[1024]{0:T(1024)S(1)} %get-tuple-element.94), channel_id=1, replica_groups=mesh['req'=32,'tp'=4] {'tp'}, dimensions={0}, use_global_device_ids=true | all-gather | bytes 20480 | tf_op jit(solution)/shard_map/all_gather | solution.py:201
  259.3 0.2 dynamic_update_slice.13
  259.4 0.3 dynamic_update_slice.14
  259.7 0.3 dynamic_update_slice.15
  260.0 0.1 sub.76
  260.1 0.1 copy.57
  260.1 0.1 sub.78
  260.2 0.8 fusion.27
  (159 shorter events, 1.8 us)
Async XLA Ops:
  7.2 9.7 %copy-start.1 = (s32[2]{0:T(128)S(1)}, s32[2]{0:T(128)}, u32[]{:S(2)}) copy-start(s32[2]{0:T(128)} %param.24) | copy-start | bytes 28
  7.2 66.4 %reduce-scatter.4.cloned.1.call-start = ((), (), s32[]{:S(2)}) async-start(), calls=%async_computation.3 | async-start | bytes 1146880
  34.0 60.0 %copy-start = (s32[64,64]{1,0:T(8,128)S(1)}, s32[64,64]{1,0:T(8,128)}, u32[]{:S(2)}) copy-start(s32[64,64]{1,0:T(8,128)} %param.30) | copy-start | bytes 49156
  34.0 60.3 %copy-start.2 = (s32[2,8,64]{2,1,0:T(8,128)S(1)}, s32[2,8,64]{2,1,0:T(8,128)}, u32[]{:S(2)}) copy-start(s32[2,8,64]{2,1,0:T(8,128)} %param.26) | copy-start | bytes 12292
  34.0 85.8 %copy-start.3 = (s32[64]{0:T(128)S(1)}, s32[64]{0:T(128)}, u32[]{:S(2)}) copy-start(s32[64]{0:T(128)} %param.31) | copy-start | bytes 772
  35.3 108.9 %all-gather.5.cloned.1.call-start = ((), (), s32[]{:S(2)}) async-start(), calls=%async_computation.2 | async-start | bytes 7569408 | tf_op jit(solution)/shard_map/all_gather | solution.py:191
  231.2 15.5 %collective-permute-start = (f32[1024]{0:T(1024)S(1)}, f32[1024]{0:T(1024)S(1)}, u32[]{:S(2)}, u32[]{:S(2)}) collective-permute-start(f32[1024]{0:T(1024)S(1)} %get-tuple-element.93), channel_id=1, source_target_pairs={{0,1},{1,2},{2,3},{3,0},{4,5},{5,6},{6,7},{7,4},{8,9},{9,10},{10,1... | collective-permute-start | bytes 12296 | tf_op jit(solution)/shard_map/ppermute | solution.py:26
  232.9 26.6 %collective-permute-start.1 = (f32[1024]{0:T(1024)S(1)}, f32[1024]{0:T(1024)S(1)}, u32[]{:S(2)}, u32[]{:S(2)}) collective-permute-start(f32[1024]{0:T(1024)S(1)} %get-tuple-element.93), channel_id=1, source_target_pairs={{0,3},{1,0},{2,1},{3,2},{4,7},{5,4},{6,5},{7,6},{8,11},{9,8},{10,9... | collective-permute-start | bytes 12296 | tf_op jit(solution)/shard_map/ppermute | solution.py:31
  246.7 13.0 %collective-permute-start.2 = (f32[1024]{0:T(1024)S(1)}, f32[1024]{0:T(1024)S(1)}, u32[]{:S(2)}, u32[]{:S(2)}) collective-permute-start(f32[1024]{0:T(1024)S(1)} %collective-permute-done), channel_id=1, source_target_pairs={{0,1},{1,2},{2,3},{3,0},{4,5},{5,6},{6,7},{7,4},{8,9},{9,10},{10,1... | collective-permute-start | bytes 12296 | tf_op jit(solution)/shard_map/ppermute | solution.py:26
Sparse Core Ops, SparseCore 0:
  35.4 38.0 reduce-scatter.3
  94.1 50.1 all-gather.4
